TPU v7x, 32 devices: a whole 2x2x4 slice. The times are simulated.
32 devices in a mesh: groups: 2 (over x), heads: 4 (over y, core), seq: 4 (over z).
Axes of the slice: x: 2, y: 2, z: 4, core: 2. Of those that a mesh axis runs over, the one named last changes fastest.
Arguments:
- lin_query: bfloat16 [4096, 4096], P(('groups', 'seq'), 'heads'), parts along dimension 0, may hold values from -6 to 6
- lin_key: bfloat16 [4096, 4096], P(('groups', 'seq'), 'heads'), parts along dimension 0, may hold values from -6 to 6
- lin_value: bfloat16 [4096, 4096], P(('groups', 'seq'), 'heads'), parts along dimension 0, may hold values from -6 to 6
- log_decay: float32 [4096, 32], P(('groups', 'seq'), 'heads'), parts along dimension 0, may hold values from -1 to 0
- stream: bfloat16 [4096, 6144], P(('groups', 'seq'), 'heads'), parts along dimension 0, may hold values from -400 to 400
- out_weight: bfloat16 [4096, 6144], P('heads', 'seq'), may hold values from -0.125 to 0.125
- norm_gain: bfloat16 [6144], P('heads'), may hold values from 0.5 to 1.5
- query_weight: bfloat16 [6144, 4096], P('seq', 'heads'), may hold values from -12 to 12
- kv_weight: bfloat16 [4, 6144, 256], P(None, 'seq'), may hold values from -1 to 1
Outputs:
- stream_next: bfloat16 [4096, 6144], P(('groups', 'seq'), 'heads'), parts along dimension 0
- attended: bfloat16 [4096, 4096], P(('groups', 'seq'), 'heads'), parts along dimension 0
There are 2 independent parts, one for each index of `groups`. A program takes and returns all parts, laid end to end along the dimension named above; an argument that names none is the same for every part. Nothing has to cross between parts.
All inputs are finite; a program needn't handle non-finite values.
Results may differ from a plain program's by a relative error of at most 0.019.
Values may be sent and summed in bfloat16 or wider, within the bound.
No kernel may reach another device: no remote copies, remote signals or barrier semaphores. Data moves between devices by JAX's collectives and lax.ppermute only.
A program may use at most 128 MiB of HBM per device.

v0:
```python
import jax
import jax.numpy as jnp
from jax import lax
from jax.sharding import PartitionSpec as P

D = 6144
QUERY_HEADS = 32
KVH = 4
DH = 128
BLOCK = 256


def from_behind(value, axis, steps):
    count = lax.axis_size(axis)
    leading, last = (max(0, -steps), min(count, count - steps))
    return lax.ppermute(value, axis, [(source, source + steps) for source in range(leading, last)])


def lightning_block(kv_state, block_inputs):
    query_blk, key_blk, value_blk, decay_blk = block_inputs
    block_len = query_blk.shape[0]
    local_cum = jnp.cumsum(decay_blk, axis=0)
    causal_mask = (jnp.arange(block_len)[:, None] >= jnp.arange(block_len)[None, :])[:, :, None]
    decay_diff = local_cum[:, None, :] - local_cum[None, :, :]
    decays = jnp.where(causal_mask, jnp.exp(jnp.where(causal_mask, decay_diff, 0.0)), 0.0)
    scores = jnp.einsum("thd,shd->hts", query_blk, key_blk, preferred_element_type=jnp.float32)
    weights = (scores * jnp.transpose(decays, (2, 0, 1))).astype(jnp.bfloat16)
    intra_out = jnp.einsum("hts,shd->thd", weights, value_blk, preferred_element_type=jnp.float32)
    query_f = query_blk.astype(jnp.float32)
    inter_out = jnp.einsum(
        "thd,hde->the",
        query_f * jnp.exp(local_cum)[:, :, None],
        kv_state,
        precision=lax.Precision.HIGHEST,
    )
    tail_decay = jnp.exp(local_cum[-1][None, :] - local_cum)
    key_f = key_blk.astype(jnp.float32) * tail_decay[:, :, None]
    kv_state = jnp.exp(local_cum[-1])[:, None, None] * kv_state + jnp.einsum(
        "shd,she->hde", key_f, value_blk.astype(jnp.float32), precision=lax.Precision.HIGHEST
    )
    return (kv_state, intra_out + inter_out)


def shards(
    lin_query, lin_key, lin_value, log_decay, stream, out_weight, norm_gain, query_weight, kv_weight
):
    tok_rows = lin_query.shape[0]
    heads_here = log_decay.shape[1]
    head_width = heads_here * DH
    nblocks = tok_rows // BLOCK
    block_shape = (nblocks, BLOCK, heads_here, DH)
    inputs = (
        lin_query.reshape(block_shape),
        lin_key.reshape(block_shape),
        lin_value.reshape(block_shape),
        log_decay.reshape(nblocks, BLOCK, heads_here),
    )
    start_state = jnp.zeros((heads_here, DH, DH), jnp.float32)
    local_state, local_out = lax.scan(lightning_block, start_state, inputs)
    local_out = local_out.reshape(tok_rows, heads_here, DH)
    decay_total = jnp.sum(log_decay, axis=0)
    totals, states = (
        lax.all_gather(decay_total[None].astype(jnp.bfloat16), "seq", axis=0, tiled=True).astype(
            jnp.float32
        ),
        lax.all_gather(local_state[None].astype(jnp.bfloat16), "seq", axis=0, tiled=True).astype(
            jnp.float32
        ),
    )
    position = lax.axis_index("seq")
    device_order = jnp.arange(totals.shape[0])
    earlier = (device_order < position)[:, None]
    before = jnp.sum(jnp.where(earlier, totals, 0.0), axis=0)
    inclusive = jnp.cumsum(totals, axis=0)
    factors = jnp.where(earlier, jnp.exp(jnp.where(earlier, before[None, :] - inclusive, 0.0)), 0.0)
    incoming = jnp.einsum("jh,jhde->hde", factors, states, precision=lax.Precision.HIGHEST)
    running = jnp.cumsum(log_decay, axis=0)
    query_f = (
        lin_query.reshape(tok_rows, heads_here, DH).astype(jnp.float32)
        * jnp.exp(running)[:, :, None]
    )
    carried = jnp.einsum("thd,hde->the", query_f, incoming, precision=lax.Precision.HIGHEST)
    lin_raw = local_out + carried
    lin_out = (
        (lin_raw * lax.rsqrt(jnp.mean(lin_raw * lin_raw, axis=-1, keepdims=True) + 1e-06))
        .astype(jnp.bfloat16)
        .reshape(tok_rows, head_width)
    )
    branch = jnp.dot(
        lin_out,
        lax.all_gather(out_weight, "seq", axis=1, tiled=True),
        preferred_element_type=jnp.float32,
    )
    kv_group = lax.axis_index("heads") * heads_here // (QUERY_HEADS // KVH)
    kv_mine = lax.dynamic_index_in_dim(kv_weight, kv_group, 0, keepdims=False)
    query_rows, kv_rows = (
        lax.all_gather(query_weight, "seq", axis=0, tiled=True),
        lax.all_gather(kv_mine, "seq", axis=0, tiled=True),
    )
    projection = jnp.concatenate([query_rows, kv_rows], axis=1)
    own_sum = lax.psum_scatter(
        branch.astype(jnp.bfloat16), "heads", scatter_dimension=1, tiled=True
    ).astype(jnp.float32)
    mixed_sum = stream.astype(jnp.float32) + own_sum
    stream_next = mixed_sum.astype(jnp.bfloat16)
    total_sq = lax.psum(jnp.sum(mixed_sum * mixed_sum, axis=1), "heads")
    normed = (
        mixed_sum
        * lax.rsqrt(total_sq / D + 1e-05)[:, None]
        * norm_gain.astype(jnp.float32)[None, :]
    ).astype(jnp.bfloat16)
    projected = jnp.dot(
        lax.all_gather(normed, "heads", axis=1, tiled=True),
        projection,
        preferred_element_type=jnp.float32,
    )
    projected = projected.astype(jnp.bfloat16)
    queries = projected[:, :head_width].reshape(tok_rows, heads_here, DH)
    keys_values = projected[:, head_width:]
    position = lax.axis_index("seq")
    query_pos = position * tok_rows + jnp.arange(tok_rows)
    score_scale = float(DH) ** (-0.5)

    def attend(state_in, kv_block, key_start):
        old_max, row_total, weighted = state_in
        key_count = kv_block.shape[0]
        key_part = kv_block[:, :DH]
        value_part = kv_block[:, DH:]
        scores = (
            jnp.einsum("thd,sd->hts", queries, key_part, preferred_element_type=jnp.float32)
            * score_scale
        )
        key_pos = key_start + jnp.arange(key_count)
        allowed = ((key_pos[None, :] <= query_pos[:, None]) & (key_pos[None, :] >= 0))[None, :, :]
        scores = jnp.where(allowed, scores, -1e30)
        new_max = jnp.maximum(old_max, jnp.max(scores, axis=-1))
        expos = jnp.where(allowed, jnp.exp(scores - new_max[:, :, None]), 0.0)
        rescale = jnp.exp(old_max - new_max)
        row_total = row_total * rescale + jnp.sum(expos, axis=-1)
        prob_bf16 = expos.astype(jnp.bfloat16)
        weighted = weighted * rescale[:, :, None] + jnp.einsum(
            "hts,sd->htd", prob_bf16, value_part, preferred_element_type=jnp.float32
        )
        return (new_max, row_total, weighted)

    initial = (
        jnp.full((heads_here, tok_rows), -1e30, jnp.float32),
        jnp.zeros((heads_here, tok_rows), jnp.float32),
        jnp.zeros((heads_here, tok_rows, DH), jnp.float32),
    )
    first_state = attend(initial, keys_values, position * tok_rows)
    seq_count = lax.axis_size("seq")

    def cycle_turn(turn_index, loop_state):
        moving, inner_state = loop_state
        moving = from_behind(moving, "seq", 1)
        source = position - turn_index
        return (moving, attend(inner_state, moving, source * tok_rows))

    _, final_state = lax.fori_loop(1, seq_count, cycle_turn, (keys_values, first_state))
    _, row_total, weighted = final_state
    attended = (
        jnp.transpose(weighted / row_total[:, :, None], (1, 0, 2))
        .reshape(tok_rows, head_width)
        .astype(jnp.bfloat16)
    )
    return (stream_next, attended)


def solution(mesh):
    return jax.shard_map(
        shards,
        mesh=mesh,
        in_specs=(
            P(("groups", "seq"), "heads"),
            P(("groups", "seq"), "heads"),
            P(("groups", "seq"), "heads"),
            P(("groups", "seq"), "heads"),
            P(("groups", "seq"), "heads"),
            P("heads", "seq"),
            P("heads"),
            P("seq", "heads"),
            P(None, "seq", None),
        ),
        out_specs=(P(("groups", "seq"), "heads"), P(("groups", "seq"), "heads")),
        check_vma=False,
    )
```

profile of v0, /device:TPU:0, one launch (start us, length us, event | category | flops | bytes accessed | tf_op | source)
XLA Modules:
  0.0 828.3 jit_solution(3079648835785859866)
XLA Ops:
  13.6 79.9 %while.34 = (s32[]{:T(128)}, f32[8,128,128]{2,1,0:T(8,128)}, f32[2,256,8,128]{1,0,3,2:T(2,128)}, f32[2,256,8]{1,2,0:T(8,128)S(1)}, bf16[2,256,8,128]{3,2,1,0:T(8...) while((s32[]{:T(128)}, f32[8,128,128]{2,1,0:T(8,128)}, ...), condition=%wide.region_3.4_spmd.clone, body=%wide.region_0.3_spmd.clone.sunk | while | flops 1078530048 | bytes 19645352 | solution.py:59
  23.9 3.8 fusion.84
  31.0 22.0 %dynamic_update_slice.6 = f32[2,256,8,128]{1,0,3,2:T(2,128)} dynamic-update-slice(f32[2,256,8,128]{1,0,3,2:T(2,128)} %get-tuple-element.452, f32[1,256,8,128]{1,0,3,2:T(1,128)} %copy.136, s32[]{:T(128)S(6)} %copy.141, s32[]{:T(128)} %constant.109.clone.1..sunk, s32[]{:T(128)} %constant.109.clone.1..sunk, s32[]{:T(128)} %constant.109.clone.1..sunk) | dynamic-update-slice | bytes 2097156 | tf_op jit(solution)/shard_map/while/body/jit(dynamic_update_index_in_dim)/dynamic_update_slice | solution.py:59
  64.5 3.8 fusion.84
  71.6 22.0 %dynamic_update_slice.6 = f32[2,256,8,128]{1,0,3,2:T(2,128)} dynamic-update-slice(f32[2,256,8,128]{1,0,3,2:T(2,128)} %get-tuple-element.452, f32[1,256,8,128]{1,0,3,2:T(1,128)} %copy.136, s32[]{:T(128)S(6)} %copy.141, s32[]{:T(128)} %constant.109.clone.1..sunk, s32[]{:T(128)} %constant.109.clone.1..sunk, s32[]{:T(128)} %constant.109.clone.1..sunk) | dynamic-update-slice | bytes 2097156 | tf_op jit(solution)/shard_map/while/body/jit(dynamic_update_index_in_dim)/dynamic_update_slice | solution.py:59
  96.3 3.9 reshape.219
  101.7 14.2 %all-reduce = bf16[32]{0:T(256)(128)(2,1)S(1)} all-reduce(bf16[32]{0:T(256)(128)(2,1)S(1)} %dynamic-update-slice), channel_id=2, replica_groups=mesh['groups'=2,'heads'=4,'seq'=4] {'seq'}, use_global_device_ids=true, to_apply=%add | all-reduce | flops 32 | bytes 128
  117.6 8.8 %all-gather.15.cloned.1.call-done = bf16[32,128,128]{2,1,0:T(8,128)(2,1)} async-done(((bf16[8,128,128]{2,1,0:T(8,128)(2,1)}), bf16[32,128,128]{2,1,0:T(8,128)(2,1)}) %all-gather.15.cloned.1.call-update) | async-done | bytes 1048592 | tf_op jit(solution)/shard_map/all_gather | solution.py:66
  127.9 4.7 multiply_reduce_fusion.2
  133.9 211.7 %all-gather.9.cloned.1.call-done = bf16[1024,6144]{1,0:T(8,128)(2,1)} async-done(((bf16[1024,1536]{1,0:T(8,128)(2,1)}), bf16[1024,6144]{1,0:T(8,128)(2,1)}) %all-gather.9.cloned.1.call-update) | async-done | bytes 12582928 | tf_op jit(solution)/shard_map/all_gather | solution.py:91
  345.6 11.8 %convolution_convert_fusion = bf16[512,6144]{1,0:T(8,128)(2,1)} fusion(bf16[512,1024]{0,1:T(8,128)(2,1)} %bitcast.181, bf16[1024,6144]{1,0:T(8,128)(2,1)} %all-gather.9.cloned.1.call-done), kind=kOutput, calls=%fused_computation.60 | convolution fusion | flops 6445596672 | bytes 19922944 | tf_op jit(solution)/shard_map/dot_general | solution.py:89
  359.1 54.5 %reduce-scatter.2.cloned.1.call-done = bf16[512,1536]{1,0:T(8,128)(2,1)} async-done(((bf16[512,6144]{1,0:T(8,128)(2,1)}), bf16[512,1536]{1,0:T(8,128)(2,1)}) %reduce-scatter.2.cloned.1.call-update) | async-done | bytes 1572880 | tf_op jit(solution)/shard_map/reduce_scatter | solution.py:101
  415.8 6.0 psum.7
  424.4 54.7 %all-gather.17.cloned.1.call-done = bf16[1,6144,256]{2,1,0:T(8,128)(2,1)} async-done(((bf16[1,1536,256]{2,1,0:T(8,128)(2,1)}), bf16[1,6144,256]{2,1,0:T(8,128)(2,1)}) %all-gather.17.cloned.1.call-update) | async-done | bytes 3145744 | tf_op jit(solution)/shard_map/all_gather | solution.py:98
  479.1 218.3 %all-gather.13.cloned.1.call-done = bf16[6144,1024]{1,0:T(8,128)(2,1)} async-done(((bf16[1536,1024]{1,0:T(8,128)(2,1)}), bf16[6144,1024]{1,0:T(8,128)(2,1)}) %all-gather.13.cloned.1.call-update) | async-done | bytes 12582928 | tf_op jit(solution)/shard_map/all_gather | solution.py:97
  697.4 46.0 %all-gather.11.cloned.1.call-done = bf16[512,6144]{1,0:T(8,128)(2,1)} async-done(((bf16[512,1536]{1,0:T(8,128)(2,1)}), bf16[512,6144]{1,0:T(8,128)(2,1)}) %all-gather.11.cloned.1.call-update) | async-done | bytes 6291472 | tf_op jit(solution)/shard_map/all_gather | solution.py:113
  743.4 15.6 %fusion.43 = bf16[512,1280]{1,0:T(8,128)(2,1)S(1)} fusion(bf16[512,6144]{1,0:T(8,128)(2,1)} %all-gather.11.cloned.1.call-done, bf16[6144,256]{1,0:T(8,128)(2,1)} %bitcast.188, bf16[6144,1024]{1,0:T(8,128)(2,1)} %all-gather.13.cloned.1.call-done), kind=kOutput, calls=%fused_computation.71 | convolution fusion | flops 8085176320 | bytes 23330816 | tf_op jit(solution)/shard_map/dot_general | solution.py:112
  762.8 3.9 fusion.49
  766.7 51.9 %while.33 = (s32[]{:T(128)}, bf16[512,256]{1,0:T(8,128)(2,1)S(1)}, f32[8,512]{1,0:T(8,128)S(1)}, f32[8,512]{1,0:T(8,128)S(1)}, f32[8,512,128]{2,1,0:T(8,128)}, /...) while((s32[]{:T(128)}, bf16[512,256]{1,0:T(8,128)(2,1)S(1)}, ...), condition=%wide.region_18.19_spmd.clone, body=%wide.region_15.18_spmd.clone.sunk | while | flops 1102587904 | bytes 50341096 | solution.py:160
  770.4 5.7 collective-permute-done
  784.2 4.4 collective-permute-start
  788.9 4.8 collective-permute-done
  801.8 4.4 collective-permute-start
  806.5 3.9 collective-permute-done
  (149 shorter events, 84.3 us)
Async XLA Ops:
  7.2 350.3 %copy-start = (bf16[4,1536,256]{2,1,0:T(8,128)(2,1)S(1)}, bf16[4,1536,256]{2,1,0:T(8,128)(2,1)}, u32[]{:S(2)}) copy-start(bf16[4,1536,256]{2,1,0:T(8,128)(2,1)} %param.21) | copy-start | bytes 9437188
  7.2 119.2 %all-gather.15.cloned.1.call-start = ((), (), s32[]{:S(2)}) async-start(), calls=%async_computation.5 | async-start | bytes 1310720 | tf_op jit(solution)/shard_map/all_gather | solution.py:66
  7.2 5.1 copy-start.6
  7.3 6.4 copy-start.9
  16.7 4.9 copy-start.2
  21.6 2.2 copy-start.3
  56.0 5.0 copy-start.2
  61.0 3.4 copy-start.3
  95.3 4.9 copy-start.11
  95.4 250.2 %all-gather.9.cloned.1.call-start = ((), (), s32[]{:S(2)}) async-start(), calls=%async_computation.1 | async-start | bytes 15728640 | tf_op jit(solution)/shard_map/all_gather | solution.py:91
  96.1 317.6 %reduce-scatter.2.cloned.1.call-start = ((), (), s32[]{:S(2)}) async-start(), calls=%async_computation.2 | async-start | bytes 7864320 | tf_op jit(solution)/shard_map/reduce_scatter | solution.py:101
  357.4 1.7 copy-start.10
  357.4 121.7 %all-gather.17.cloned.1.call-start = ((), (), s32[]{:S(2)}) async-start(), calls=%async_computation.6 | async-start | bytes 3932160 | tf_op jit(solution)/shard_map/all_gather | solution.py:98
  358.4 55.2 %copy-start.4 = (bf16[512,1536]{1,0:T(8,128)(2,1)S(1)}, bf16[512,1536]{1,0:T(8,128)(2,1)}, u32[]{:S(2)}) copy-start(bf16[512,1536]{1,0:T(8,128)(2,1)} %param.17) | copy-start | bytes 4718596
  358.5 338.9 %all-gather.13.cloned.1.call-start = ((), (), s32[]{:S(2)}) async-start(), calls=%async_computation.4 | async-start | bytes 15728640 | tf_op jit(solution)/shard_map/all_gather | solution.py:97
  359.1 384.3 %all-gather.11.cloned.1.call-start = ((), (), s32[]{:S(2)}) async-start(), calls=%async_computation.3 | async-start | bytes 7864320 | tf_op jit(solution)/shard_map/all_gather | solution.py:113
  413.7 8.1 copy-start.5
  766.7 9.3 %collective-permute-start = (bf16[512,256]{1,0:T(8,128)(2,1)S(1)}, bf16[512,256]{1,0:T(8,128)(2,1)S(1)}, u32[]{:S(2)}, u32[]{:S(2)}) collective-permute-start(bf16[512,256]{1,0:T(8,128)(2,1)S(1)} %get-tuple-element.481), channel_id=1, source_target_pairs={{0,1},{1,2},{2,3},{4,5},{5,6},{6,7},{8,9},{9,10},{10,11},{12,13},{... | collective-permute-start | bytes 786440 | tf_op jit(solution)/shard_map/while/body/eval_jaxpr/ppermute | solution.py:16
  777.6 2.1 copy-start.7
  784.2 9.5 %collective-permute-start = (bf16[512,256]{1,0:T(8,128)(2,1)S(1)}, bf16[512,256]{1,0:T(8,128)(2,1)S(1)}, u32[]{:S(2)}, u32[]{:S(2)}) collective-permute-start(bf16[512,256]{1,0:T(8,128)(2,1)S(1)} %get-tuple-element.481), channel_id=1, source_target_pairs={{0,1},{1,2},{2,3},{4,5},{5,6},{6,7},{8,9},{9,10},{10,11},{12,13},{... | collective-permute-start | bytes 786440 | tf_op jit(solution)/shard_map/while/body/eval_jaxpr/ppermute | solution.py:16
  795.2 2.1 copy-start.7
  801.8 8.6 %collective-permute-start = (bf16[512,256]{1,0:T(8,128)(2,1)S(1)}, bf16[512,256]{1,0:T(8,128)(2,1)S(1)}, u32[]{:S(2)}, u32[]{:S(2)}) collective-permute-start(bf16[512,256]{1,0:T(8,128)(2,1)S(1)} %get-tuple-element.481), channel_id=1, source_target_pairs={{0,1},{1,2},{2,3},{4,5},{5,6},{6,7},{8,9},{9,10},{10,11},{12,13},{... | collective-permute-start | bytes 786440 | tf_op jit(solution)/shard_map/while/body/eval_jaxpr/ppermute | solution.py:16
  812.0 2.1 copy-start.7
  818.6 2.9 copy-start.1
  (3 other events, 4.1 us)
Sparse Core Ops, SparseCore 0:
  95.5 30.8 all-gather.14
  127.9 217.6 all-gather.8
  357.5 56.0 reduce-scatter.1
  415.7 63.4 all-gather.16
  480.5 216.8 all-gather.12
  698.8 44.5 all-gather.10
where the time goes:
time: 832 us; the launch traced here: 828 us
  waiting for transfers between devices  610 us (73%)
  local copies, waits for them, and re-layouts  74.6 us (9%)
  matrix products  71.7 us (9%)
  other arithmetic  24.5 us (3%)
  blocking collectives  20.1 us (2%)
  between operations  15 us (2%)
  starting transfers between devices  12.4 us (1%)
    all_gather x1, waiting for transfers between devices, shards(): lax.all_gather(query_weight, 'seq', axis=0, tiled=True)  218 us
    all_gather x1, waiting for transfers between devices, shards(): lax.all_gather(out_weight, 'seq', axis=1, tiled=True)  212 us
    all_gather x1, waiting for transfers between devices, shards(): lax.all_gather(kv_mine, 'seq', axis=0, tiled=True)  54.7 us
    reduce_scatter x1, waiting for transfers between devices, shards(): lax.psum_scatter(branch.astype(jnp.bfloat16), 'heads', scatter_dimension=...  54.5 us
    dynamic_update_slice x4, local copies, waits for them, and re-layouts, shards(): local_state, local_out = lax.scan(lightning_block, start_state, inputs)  50.5 us
    all_gather x1, waiting for transfers between devices, shards(): lax.all_gather(normed, 'heads', axis=1, tiled=True)  46 us
  transfers between devices with their start and end apart: 9, of which 9 were waited for; matrix products, arithmetic and copies ran while one was open for 2% of the time, Pallas kernels for 0%

commit v1 on v0

--- a/solution.py
+++ b/solution.py
@@ -8,6 +8,24 @@
 KVH = 4
 DH = 128
 BLOCK = 256
+
+
+def ring_gather(value, axis, dim):
+    ways, here, step = (lax.axis_size(axis), lax.axis_index(axis), value.shape[dim])
+    lengths = [n * ways if d == dim else n for d, n in enumerate(value.shape)]
+    full = lax.dynamic_update_slice_in_dim(
+        jnp.zeros(lengths, value.dtype), value, here * step, axis=dim
+    )
+    going_up = going_down = value
+    for far in range(1, ways // 2 + 1):
+        going_up = lax.ppermute(going_up, axis, [(d, (d + 1) % ways) for d in range(ways)])
+        full = lax.dynamic_update_slice_in_dim(full, going_up, (here - far) % ways * step, axis=dim)
+        if 2 * far < ways:
+            going_down = lax.ppermute(going_down, axis, [(d, (d - 1) % ways) for d in range(ways)])
+            full = lax.dynamic_update_slice_in_dim(
+                full, going_down, (here + far) % ways * step, axis=dim
+            )
+    return full
 
 
 def from_behind(value, axis, steps):
@@ -110,9 +128,7 @@
         * norm_gain.astype(jnp.float32)[None, :]
     ).astype(jnp.bfloat16)
     projected = jnp.dot(
-        lax.all_gather(normed, "heads", axis=1, tiled=True),
-        projection,
-        preferred_element_type=jnp.float32,
+        ring_gather(normed, "heads", 1), projection, preferred_element_type=jnp.float32
     )
     projected = projected.astype(jnp.bfloat16)
     queries = projected[:, :head_width].reshape(tok_rows, heads_here, DH)

time: 832 us -> 784 us (0.942)
  waiting for transfers between devices: 610 us -> 553 us
  local copies, waits for them, and re-layouts: 74.6 us -> 83.2 us
    all_gather x1, waiting for transfers between devices: 54.7 us -> 0.01 us  [shards(): lax.all_gather(kv_mine, 'seq', axis=0, tiled=True)]
    ppermute x0 -> x3, waiting for transfers between devices: none -> 49.4 us  [the longest x2 49.4 us: ring_gather(): lax.ppermute(going_up, axis, [(d, (d + 1) % ways) for d in range(ways)])]
    all_gather x1 -> x0, waiting for transfers between devices: 46 us -> none  [shards(): lax.all_gather(normed, 'heads', axis=1, tiled=True)]
  transfers between devices with their start and end apart: 9 -> 11, of which waited for: 9 -> 9; matrix products, arithmetic and copies ran while one was open for 2% -> 4% of each run, Pallas kernels for 0% -> 0%
where the time goes in v1:
time: 784 us; the launch traced here: 780 us
  waiting for transfers between devices  553 us (71%)
  local copies, waits for them, and re-layouts  83.2 us (11%)
  matrix products  71.6 us (9%)
  other arithmetic  25.7 us (3%)
  blocking collectives  19.9 us (3%)
  between operations  14.6 us (2%)
  starting transfers between devices  12 us (2%)
    all_gather x1, waiting for transfers between devices, shards(): lax.all_gather(query_weight, 'seq', axis=0, tiled=True)  212 us
    all_gather x1, waiting for transfers between devices, shards(): lax.all_gather(out_weight, 'seq', axis=1, tiled=True)  212 us
    reduce_scatter x1, waiting for transfers between devices, shards(): lax.psum_scatter(branch.astype(jnp.bfloat16), 'heads', scatter_dimension=...  54.6 us
    dynamic_update_slice x4, local copies, waits for them, and re-layouts, shards(): local_state, local_out = lax.scan(lightning_block, start_state, inputs)  50.5 us
    ppermute x2, waiting for transfers between devices, ring_gather(): lax.ppermute(going_up, axis, [(d, (d + 1) % ways) for d in range(ways)])  49.4 us
  transfers between devices with their start and end apart: 11, of which 9 were waited for; matrix products, arithmetic and copies ran while one was open for 4% of the time, Pallas kernels for 0%

profile of v1, /device:TPU:0, one launch (start us, length us, event | category | flops | bytes accessed | tf_op | source)
XLA Modules:
  0.0 780.2 jit_solution(14996494444628762085)
XLA Ops:
  13.6 79.9 %while.34 = (s32[]{:T(128)}, f32[8,128,128]{2,1,0:T(8,128)}, f32[2,256,8,128]{1,0,3,2:T(2,128)}, f32[2,256,8]{1,2,0:T(8,128)S(1)}, bf16[2,256,8,128]{3,2,1,0:T(8...) while((s32[]{:T(128)}, f32[8,128,128]{2,1,0:T(8,128)}, ...), condition=%wide.region_3.4_spmd.clone, body=%wide.region_0.3_spmd.clone.sunk | while | flops 1078530048 | bytes 19645352 | solution.py:77
  23.9 3.8 fusion.84
  31.0 22.0 %dynamic_update_slice.26 = f32[2,256,8,128]{1,0,3,2:T(2,128)} dynamic-update-slice(f32[2,256,8,128]{1,0,3,2:T(2,128)} %get-tuple-element.454, f32[1,256,8,128]{1,0,3,2:T(1,128)} %copy.136, s32[]{:T(128)S(6)} %copy.141, s32[]{:T(128)} %constant.133.clone.1..sunk, s32[]{:T(128)} %constant.133.clone.1..sunk, s32[]{:T(128)} %constant.133.clone.1..sunk) | dynamic-update-slice | bytes 2097156 | tf_op jit(solution)/shard_map/while/body/jit(dynamic_update_index_in_dim)/dynamic_update_slice | solution.py:77
  64.5 3.8 fusion.84
  71.6 22.0 %dynamic_update_slice.26 = f32[2,256,8,128]{1,0,3,2:T(2,128)} dynamic-update-slice(f32[2,256,8,128]{1,0,3,2:T(2,128)} %get-tuple-element.454, f32[1,256,8,128]{1,0,3,2:T(1,128)} %copy.136, s32[]{:T(128)S(6)} %copy.141, s32[]{:T(128)} %constant.133.clone.1..sunk, s32[]{:T(128)} %constant.133.clone.1..sunk, s32[]{:T(128)} %constant.133.clone.1..sunk) | dynamic-update-slice | bytes 2097156 | tf_op jit(solution)/shard_map/while/body/jit(dynamic_update_index_in_dim)/dynamic_update_slice | solution.py:77
  96.3 3.9 reshape.219
  101.7 14.2 %all-reduce = bf16[32]{0:T(256)(128)(2,1)S(1)} all-reduce(bf16[32]{0:T(256)(128)(2,1)S(1)} %dynamic-update-slice), channel_id=2, replica_groups=mesh['groups'=2,'heads'=4,'seq'=4] {'seq'}, use_global_device_ids=true, to_apply=%add | all-reduce | flops 32 | bytes 128
  117.6 8.8 %all-gather.12.cloned.1.call-done = bf16[32,128,128]{2,1,0:T(8,128)(2,1)} async-done(((bf16[8,128,128]{2,1,0:T(8,128)(2,1)}), bf16[32,128,128]{2,1,0:T(8,128)(2,1)}) %all-gather.12.cloned.1.call-update) | async-done | bytes 1048592 | tf_op jit(solution)/shard_map/all_gather | solution.py:84
  127.9 4.7 multiply_reduce_fusion.2
  133.9 211.7 %all-gather.8.cloned.1.call-done = bf16[1024,6144]{1,0:T(8,128)(2,1)} async-done(((bf16[1024,1536]{1,0:T(8,128)(2,1)}), bf16[1024,6144]{1,0:T(8,128)(2,1)}) %all-gather.8.cloned.1.call-update) | async-done | bytes 12582928 | tf_op jit(solution)/shard_map/all_gather | solution.py:109
  345.6 11.7 %convolution_convert_fusion = bf16[512,6144]{1,0:T(8,128)(2,1)} fusion(bf16[512,1024]{0,1:T(8,128)(2,1)} %bitcast.181, bf16[1024,6144]{1,0:T(8,128)(2,1)} %all-gather.8.cloned.1.call-done), kind=kOutput, calls=%fused_computation.60 | convolution fusion | flops 6445596672 | bytes 19922944 | tf_op jit(solution)/shard_map/dot_general | solution.py:107
  359.0 54.6 %reduce-scatter.2.cloned.1.call-done = bf16[512,1536]{1,0:T(8,128)(2,1)} async-done(((bf16[512,6144]{1,0:T(8,128)(2,1)}), bf16[512,1536]{1,0:T(8,128)(2,1)}) %reduce-scatter.2.cloned.1.call-update) | async-done | bytes 1572880 | tf_op jit(solution)/shard_map/reduce_scatter | solution.py:119
  416.7 5.7 psum.7
  429.9 33.7 %collective-permute-done.1 = bf16[512,1536]{1,0:T(8,128)(2,1)S(1)} collective-permute-done((bf16[512,1536]{1,0:T(8,128)(2,1)}, bf16[512,1536]{1,0:T(8,128)(2,1)S(1)}, u32[]{:S(2)}, u32[]{:S(2)}) %collective-permute-start.1) | collective-permute-done | bytes 1572896 | tf_op jit(solution)/shard_map/ppermute | solution.py:21
  467.9 15.6 %collective-permute-done.3 = bf16[512,1536]{1,0:T(8,128)(2,1)S(1)} collective-permute-done((bf16[512,1536]{1,0:T(8,128)(2,1)S(1)}, bf16[512,1536]{1,0:T(8,128)(2,1)S(1)}, u32[]{:S(2)}, u32[]{:S(2)}) %collective-permute-start.3) | collective-permute-done | bytes 1572896 | tf_op jit(solution)/shard_map/ppermute | solution.py:21
  484.9 212.5 %all-gather.10.cloned.1.call-done = bf16[6144,1024]{1,0:T(8,128)(2,1)} async-done(((bf16[1536,1024]{1,0:T(8,128)(2,1)}), bf16[6144,1024]{1,0:T(8,128)(2,1)}) %all-gather.10.cloned.1.call-update) | async-done | bytes 12582928 | tf_op jit(solution)/shard_map/all_gather | solution.py:115
  697.4 15.6 %fusion.43 = bf16[512,1280]{1,0:T(8,128)(2,1)S(1)} fusion(bf16[512,6144]{1,0:T(8,128)(2,1)} %constant_dynamic-update-slice_fusion, bf16[6144,256]{1,0:T(8,128)(2,1)} %bitcast.188, bf16[6144,1024]{1,0:T(8,128)(2,1)} %all-gather.10.cloned.1.call-done), kind=kOutput, calls=%fused_computation.71 | convolution fusion | flops 8085176320 | bytes 23330816 | tf_op jit(solution)/shard_map/dot_general | solution.py:130
  717.0 3.9 fusion.49
  720.9 49.9 %while.33 = (s32[]{:T(128)}, bf16[512,256]{1,0:T(8,128)(2,1)S(1)}, f32[8,512]{1,0:T(8,128)S(1)}, f32[8,512]{1,0:T(8,128)S(1)}, f32[8,512,128]{2,1,0:T(8,128)}, /...) while((s32[]{:T(128)}, bf16[512,256]{1,0:T(8,128)(2,1)S(1)}, ...), condition=%wide.region_18.19_spmd.clone, body=%wide.region_15.18_spmd.clone.sunk | while | flops 1102587904 | bytes 50341096 | solution.py:176
  722.5 5.7 collective-permute-done
  736.4 4.4 collective-permute-start
  741.0 4.8 collective-permute-done
  754.0 4.4 collective-permute-start
  758.7 4.0 collective-permute-done
  (156 shorter events, 93.8 us)
Async XLA Ops:
  7.2 350.3 %copy-start = (bf16[4,1536,256]{2,1,0:T(8,128)(2,1)S(1)}, bf16[4,1536,256]{2,1,0:T(8,128)(2,1)}, u32[]{:S(2)}) copy-start(bf16[4,1536,256]{2,1,0:T(8,128)(2,1)} %param.21) | copy-start | bytes 9437188
  7.2 119.2 %all-gather.12.cloned.1.call-start = ((), (), s32[]{:S(2)}) async-start(), calls=%async_computation.4 | async-start | bytes 1310720 | tf_op jit(solution)/shard_map/all_gather | solution.py:84
  7.2 5.1 copy-start.6
  7.3 6.4 copy-start.9
  16.7 4.9 copy-start.2
  21.6 2.2 copy-start.3
  56.0 5.0 copy-start.2
  61.0 3.4 copy-start.3
  95.3 4.9 copy-start.11
  95.4 250.2 %all-gather.8.cloned.1.call-start = ((), (), s32[]{:S(2)}) async-start(), calls=%async_computation.1 | async-start | bytes 15728640 | tf_op jit(solution)/shard_map/all_gather | solution.py:109
  96.1 317.5 %reduce-scatter.2.cloned.1.call-start = ((), (), s32[]{:S(2)}) async-start(), calls=%async_computation.2 | async-start | bytes 7864320 | tf_op jit(solution)/shard_map/reduce_scatter | solution.py:119
  357.4 127.5 %all-gather.14.cloned.1.call-start = ((), (), s32[]{:S(2)}) async-start(), calls=%async_computation.5 | async-start | bytes 3932160 | tf_op jit(solution)/shard_map/all_gather | solution.py:116
  358.4 55.2 %copy-start.4 = (bf16[512,1536]{1,0:T(8,128)(2,1)S(1)}, bf16[512,1536]{1,0:T(8,128)(2,1)}, u32[]{:S(2)}) copy-start(bf16[512,1536]{1,0:T(8,128)(2,1)} %param.17) | copy-start | bytes 4718596
  358.4 338.9 %all-gather.10.cloned.1.call-start = ((), (), s32[]{:S(2)}) async-start(), calls=%async_computation.3 | async-start | bytes 15728640 | tf_op jit(solution)/shard_map/all_gather | solution.py:115
  422.5 3.4 copy-start.5
  428.2 35.5 %collective-permute-start.1 = (bf16[512,1536]{1,0:T(8,128)(2,1)}, bf16[512,1536]{1,0:T(8,128)(2,1)S(1)}, u32[]{:S(2)}, u32[]{:S(2)}) collective-permute-start(bf16[512,1536]{1,0:T(8,128)(2,1)} %get-tuple-element.315), channel_id=1, source_target_pairs={{0,4},{4,8},{8,12},{12,0},{1,5},{5,9},{9,13},{13,1},{2,6},{6,10},{... | collective-permute-start | bytes 4718600 | tf_op jit(solution)/shard_map/ppermute | solution.py:21
  428.2 37.0 %collective-permute-start.2 = (bf16[512,1536]{1,0:T(8,128)(2,1)}, bf16[512,1536]{1,0:T(8,128)(2,1)}, u32[]{:S(2)}, u32[]{:S(2)}) collective-permute-start(bf16[512,1536]{1,0:T(8,128)(2,1)} %get-tuple-element.315), channel_id=1, source_target_pairs={{0,12},{4,0},{8,4},{12,8},{1,13},{5,1},{9,5},{13,9},{2,14},{6,2},{... | collective-permute-start | bytes 4718600 | tf_op jit(solution)/shard_map/ppermute | solution.py:24
  463.7 19.8 %collective-permute-start.3 = (bf16[512,1536]{1,0:T(8,128)(2,1)S(1)}, bf16[512,1536]{1,0:T(8,128)(2,1)S(1)}, u32[]{:S(2)}, u32[]{:S(2)}) collective-permute-start(bf16[512,1536]{1,0:T(8,128)(2,1)S(1)} %collective-permute-done.1), channel_id=1, source_target_pairs={{0,4},{4,8},{8,12},{12,0},{1,5},{5,9},{9,13},{13,1},{2,6},{6,10},{... | collective-permute-start | bytes 4718600 | tf_op jit(solution)/shard_map/ppermute | solution.py:21
  721.0 7.3 collective-permute-start
  729.8 2.1 copy-start.7
  736.4 9.5 %collective-permute-start = (bf16[512,256]{1,0:T(8,128)(2,1)S(1)}, bf16[512,256]{1,0:T(8,128)(2,1)S(1)}, u32[]{:S(2)}, u32[]{:S(2)}) collective-permute-start(bf16[512,256]{1,0:T(8,128)(2,1)S(1)} %get-tuple-element.483), channel_id=1, source_target_pairs={{0,1},{1,2},{2,3},{4,5},{5,6},{6,7},{8,9},{9,10},{10,11},{12,13},{... | collective-permute-start | bytes 786440 | tf_op jit(solution)/shard_map/while/body/eval_jaxpr/ppermute | solution.py:34
  747.4 2.1 copy-start.7
  754.0 8.7 %collective-permute-start = (bf16[512,256]{1,0:T(8,128)(2,1)S(1)}, bf16[512,256]{1,0:T(8,128)(2,1)S(1)}, u32[]{:S(2)}, u32[]{:S(2)}) collective-permute-start(bf16[512,256]{1,0:T(8,128)(2,1)S(1)} %get-tuple-element.483), channel_id=1, source_target_pairs={{0,1},{1,2},{2,3},{4,5},{5,6},{6,7},{8,9},{9,10},{10,11},{12,13},{... | collective-permute-start | bytes 786440 | tf_op jit(solution)/shard_map/while/body/eval_jaxpr/ppermute | solution.py:34
  770.8 2.9 copy-start.1
  (5 other events, 7.8 us)
Sparse Core Ops, SparseCore 0:
  95.5 30.8 all-gather.11
  127.9 217.6 all-gather.7
  357.5 56.0 reduce-scatter.1
  415.6 63.4 all-gather.13
  480.5 216.8 all-gather.9
